TPU v7x, 32 devices: a whole 2x2x4 slice. The times are simulated.
32 devices in a mesh: layer: 4 (over y, x), tok: 8 (over z, core).
Axes of the slice: x: 2, y: 2, z: 4, core: 2. Of those that a mesh axis runs over, the one named last changes fastest.
Arguments:
- residual: bfloat16 [4, 1024, 3584], P('layer', 'tok'), may hold values from -6 to 6
- targets: bfloat16 [4, 1024, 3584], P('layer', 'tok'), may hold values from -6 to 6
- block_ids: int32 [4, 1024, 2], P(None, 'tok'), may hold values from 0 to 127, all different within a row; in each aligned block of 128 rows (0 to 127, 128 to 255, ..., all dimensions but the last counted through in order) at most 4 rows name the same one
- encoder_weight: bfloat16 [4, 3584, 16384], P('layer', None, 'tok'), may hold values from -0.09375 to 0.09375
- encoder_bias: float32 [4, 16384], P('layer', 'tok'), may hold values from -3 to 3
- decoder_weight: bfloat16 [4, 4, 16384, 3584], P('layer', None, 'tok'), may hold values from -0.25 to 0.25
- decoder_bias: float32 [4, 3584], P('layer'), may hold values from -3 to 3
Outputs:
- reconstruction: bfloat16 [4, 1024, 3584], P('layer', 'tok')
- error: float32 [4, 1024], P('layer', 'tok')
Inputs may be any that keep to these rules, and one draw needn't show every extreme that they name: `block_ids`: A token's 2 blocks in a layer are distinct. In each layer, the 128 rows of one device (aligned blocks of tokens) name no block more than 4 times, and some block exactly 4 times.
All inputs are finite; a program needn't handle non-finite values.
Results may differ from a plain program's by a relative error of at most 0.0053.
Values may be sent and summed in bfloat16 or wider, within the bound.
No kernel may reach another device: no remote copies, remote signals or barrier semaphores. Data moves between devices by JAX's collectives and lax.ppermute only.
A program may use at most 192 MiB of HBM per device.

v0:
```python
import jax
import jax.numpy as jnp
from jax import lax
from jax.sharding import PartitionSpec as P

BLOCK = 128


def owner_tables(ids_all, owner, per_owner, capacity, tokens):
    layers, _, topk = ids_all.shape
    local = ids_all.reshape(layers, tokens * topk) - owner * per_owner
    owned = (local >= 0) & (local < per_owner)
    onehot = (local[..., None] == jnp.arange(per_owner, dtype=jnp.int32)).astype(jnp.int32)
    rank = jnp.sum((jnp.cumsum(onehot, axis=1) - onehot) * onehot, axis=2)
    slot_count = per_owner * capacity
    slot = jnp.where(owned, local * capacity + rank, slot_count)
    token_of = jnp.arange(tokens * topk, dtype=jnp.int32) // topk
    empty = jnp.full((slot_count,), tokens, jnp.int32)
    return jax.vmap(lambda s: empty.at[s].set(token_of, mode="drop"))(slot)


def body(residual, targets, block_ids, encoder_weight, encoder_bias, decoder_weight, decoder_bias):
    layer_index = lax.axis_index("layer")
    tok_index = lax.axis_index("tok")
    layers = lax.axis_size("layer")
    tok_count = lax.axis_size("tok")
    tok_rows = residual.shape[1]
    width = residual.shape[2]
    topk = block_ids.shape[2]
    per_owner = encoder_weight.shape[2] // BLOCK
    blocks = per_owner * tok_count
    capacity = max(2, 2 * tok_rows * topk // blocks) * tok_count
    slot_count = per_owner * capacity
    tokens = tok_rows * tok_count
    ids_all = lax.all_gather(block_ids, "tok", axis=1, tiled=True)
    table = owner_tables(ids_all, tok_index, per_owner, capacity, tokens)
    res_all = lax.all_gather(residual[0], "tok", axis=0, tiled=True)
    own_table = lax.dynamic_index_in_dim(table, layer_index, 0, keepdims=False)
    rows = jnp.take(res_all, jnp.minimum(own_table, tokens - 1), axis=0)
    enc_blocks = encoder_weight[0].reshape(width, per_owner, BLOCK)
    pre = jnp.einsum(
        "bcd,dbe->bce",
        rows.reshape(per_owner, capacity, width),
        enc_blocks,
        preferred_element_type=jnp.float32,
    )
    pre = pre + encoder_bias[0].reshape(per_owner, 1, BLOCK)
    codes = jnp.maximum(pre, 0.0).astype(jnp.bfloat16)
    all_codes = lax.all_gather(codes, "layer", axis=0, tiled=False)
    terms = jnp.einsum(
        "sbce,sbed->sbcd",
        all_codes,
        decoder_weight[0].reshape(layers, per_owner, BLOCK, width),
        preferred_element_type=jnp.float32,
    ).astype(jnp.bfloat16)
    valid = jnp.arange(layers, dtype=jnp.int32) <= layer_index
    scatter = (table[:, :, None] == jnp.arange(tokens, dtype=jnp.int32)[None, None, :]) & valid[
        :, None, None
    ]
    partial = jnp.einsum(
        "sct,scd->td",
        scatter.astype(jnp.bfloat16),
        terms.reshape(layers, slot_count, width),
        preferred_element_type=jnp.float32,
    )
    summed = lax.psum_scatter(partial.astype(jnp.bfloat16), "tok", scatter_dimension=0, tiled=True)
    recon32 = decoder_bias[0][None, :] + summed.astype(jnp.float32)
    difference = recon32 - targets[0].astype(jnp.float32)
    error = jnp.mean(difference * difference, axis=1)
    return (recon32.astype(jnp.bfloat16)[None], error[None])


def solution(mesh):
    in_specs = (
        P("layer", "tok", None),
        P("layer", "tok", None),
        P(None, "tok", None),
        P("layer", None, "tok"),
        P("layer", "tok"),
        P("layer", None, "tok", None),
        P("layer", None),
    )
    out_specs = (P("layer", "tok", None), P("layer", "tok"))
    return jax.shard_map(body, mesh=mesh, in_specs=in_specs, out_specs=out_specs, check_vma=False)
```

profile of v0, /device:TPU:0, one launch (start us, length us, event | category | flops | bytes accessed | tf_op | source)
XLA Modules:
  0.0 264.9 jit_solution(11410956164858787547)
XLA Ops:
  7.2 0.0 copy-start.3
  7.2 0.0 copy-start.2
  7.2 0.0 all-gather.4.cloned.1.call-start
  7.2 0.7 all-gather.4.cloned.1.call-update
  7.9 0.0 reduce-scatter.2.cloned.1.call-start
  8.0 13.8 %all_gather.12 = s32[4,1024,2]{1,2,0:T(2,128)S(1)} all-gather(s32[4,128,2]{1,2,0:T(2,128)} %param.9), channel_id=1, replica_groups=mesh['layer'=4,'tok'=8] {'tok'}, dimensions={1}, use_global_device_ids=true | all-gather | bytes 36864 | tf_op jit(solution)/shard_map/all_gather | solution.py:35
  21.8 0.6 copy.20
  22.3 0.3 copy.23
  22.7 0.1 fusion.30
  22.7 18.1 %reduce-window.6 = s32[4,16,16,128]{3,2,1,0:T(8,128)S(1)} reduce-window(s32[4,16,16,128]{3,2,1,0:T(8,128)S(1)} %fusion.30, s32[]{:T(128)} %constant.55.clone.1), window={size=1x1x1x128 pad=0_0x0_0x0_0x127_0}, to_apply=%region_0.0 | reduce-window | flops 16646144 | bytes 1048580 | tf_op jit(solution)/shard_map/reduce-window
  40.9 1.3 slice_reduce_fusion
  42.2 0.7 reduce-window.9
  42.9 0.2 broadcast_add_fusion
  43.1 0.1 reduce_window_sum.16
  43.2 0.3 copy.21
  43.6 0.8 copy.18
  44.4 1.6 and.37
  46.0 0.6 copy.19
  46.6 0.3 copy.24
  46.9 0.2 fusion.29
  47.1 0.0 copy-done.3
  47.1 0.1 multiply_reduce_fusion
  47.2 0.0 copy-done.2
  47.2 0.1 and_reduce_fusion
  47.4 30.4 %scatter_custom_fusion = s32[2048]{0:T(1024)S(1)} fusion(s32[8192]{0:T(1024)S(1)} %bitcast.59, s32[8192]{0:T(1024)S(1)} %bitcast.60, s32[]{:T(128)} %constant.30.clone.1), kind=kCustom, calls=%fused_computation.52 | custom fusion | bytes 8196
  77.9 0.1 min.26
  78.0 14.5 %copy.28 = bf16[448,8,16,128]{3,2,1,0:T(8,128)(2,1)} copy(bf16[448,8,16,128]{3,1,2,0:T(8,128)(2,1)} %bitcast.51) | data formatting | bytes 29360128
  92.6 0.0 all-gather.4.cloned.1.call-done
  92.6 0.0 copy-start.4
  92.6 12.0 %gather_fusion = bf16[512,3584]{1,0:T(8,128)(2,1)} fusion(bf16[1024,3584]{1,0:T(8,128)(2,1)} %bitcast.48, s32[1024]{0:T(1024)S(1)} %pad_clamp_fusion), kind=kCustom, calls=%fused_computation | custom fusion | bytes 7342080 | tf_op jit(solution)/shard_map/jit(_take)/gather | solution.py:39
  104.6 0.0 copy-done.4
  104.6 15.1 %fusion.22 = bf16[16,32,128]{2,1,0:T(8,128)(2,1)S(1)} fusion(bf16[3584,16,128]{2,1,0:T(8,128)(2,1)} %bitcast.52, bf16[16,32,3584]{2,1,0:T(8,128)(2,1)} %bitcast.56, pred[16,32]{1,0:T(8,128)(4,1)S(1)} %compare_and_fusion.1, f32[16,128]{1,0:T(8,128)S(1)} %bitcast.62), kind=kOutput, calls=%fused_computation.20 | convolution fusion | flops 471793664 | bytes 18489856 | tf_op jit(solution)/shard_map/bcd,dbe->bce/dot_general | solution.py:41
  119.7 10.4 %all-gather.1 = bf16[64,32,128]{2,1,0:T(8,128)(2,1)S(1)} all-gather(bf16[16,32,128]{2,1,0:T(8,128)(2,1)S(1)} %fusion.22), channel_id=3, replica_groups=mesh['layer'=4,'tok'=8] {'layer'}, dimensions={0}, use_global_device_ids=true | all-gather | bytes 655360 | tf_op jit(solution)/shard_map/all_gather | solution.py:49
  130.1 26.1 %convolution_convert_fusion = bf16[4,16,32,3584]{3,2,1,0:T(8,128)(2,1)} fusion(bf16[4,16,32,128]{3,2,1,0:T(8,128)(2,1)S(1)} %bitcast.57, bf16[4,16,128,3584]{3,2,1,0:T(8,128)(2,1)} %bitcast.49), kind=kOutput, calls=%fused_computation.5 | convolution fusion | flops 1886388224 | bytes 73924608 | tf_op jit(solution)/shard_map/sbce,sbed->sbcd/dot_general | solution.py:50
  156.3 21.6 %bitcast_convert_fusion = bf16[1024,3584]{1,0:T(8,128)(2,1)} fusion(bf16[4,512,3584]{2,1,0:T(8,128)(2,1)} %bitcast.50, s32[4,512]{1,0:T(4,128)S(1)} %reshape.136, pred[4]{0:T(512)(128)(4,1)S(1)} %iota_compare_fusion.3), kind=kOutput, calls=%fused_computation.2 | convolution fusion | flops 15040249856 | bytes 22028292 | tf_op jit(solution)/shard_map/sct,scd->td/dot_general | solution.py:60
  177.9 0.0 copy-start.1
  177.9 0.0 copy-start
  177.9 0.0 reduce-scatter.2.cloned.1.call-update
  177.9 0.7 copy-done.1
  178.6 76.4 %reduce-scatter.2.cloned.1.call-done = bf16[128,3584]{1,0:T(8,128)(2,1)} async-done(((bf16[1024,3584]{1,0:T(8,128)(2,1)}), bf16[128,3584]{1,0:T(8,128)(2,1)}) %reduce-scatter.2.cloned.1.call-update) | async-done | bytes 917520 | tf_op jit(solution)/shard_map/reduce_scatter | solution.py:66
  255.0 0.0 copy-done
  255.0 2.5 fusion.9
  257.5 0.5 multiply_bitcast_fusion
  (16 shorter events, 0.2 us)
Async XLA Ops:
  7.2 40.0 %copy-start.3 = (s32[2]{0:T(128)S(1)}, s32[2]{0:T(128)}, u32[]{:S(2)}) copy-start(s32[2]{0:T(128)} %constant.72) | copy-start | bytes 28
  7.2 40.1 %copy-start.2 = (s32[2]{0:T(128)S(1)}, s32[2]{0:T(128)}, u32[]{:S(2)}) copy-start(s32[2]{0:T(128)} %constant.75) | copy-start | bytes 28
  7.2 85.4 %all-gather.4.cloned.1.call-start = ((), (), s32[]{:S(2)}) async-start(), calls=%async_computation.2 | async-start | bytes 8257536 | tf_op jit(solution)/shard_map/all_gather | solution.py:37
  7.9 247.1 %reduce-scatter.2.cloned.1.call-start = ((), (), s32[]{:S(2)}) async-start(), calls=%async_computation.1 | async-start | bytes 8257536 | tf_op jit(solution)/shard_map/reduce_scatter | solution.py:66
  92.6 12.0 %copy-start.4 = (f32[1,2048]{1,0:T(1,128)S(1)}, f32[1,2048]{1,0:T(1,128)}, u32[]{:S(2)}) copy-start(f32[1,2048]{1,0:T(1,128)} %param.11) | copy-start | bytes 24580
  177.9 0.7 copy-start.1
  177.9 77.1 %copy-start = (bf16[1,128,3584]{2,1,0:T(8,128)(2,1)S(1)}, bf16[1,128,3584]{2,1,0:T(8,128)(2,1)}, u32[]{:S(2)}) copy-start(bf16[1,128,3584]{2,1,0:T(8,128)(2,1)} %param.8) | copy-start | bytes 2752516
Sparse Core Ops, SparseCore 0:
  9.7 76.0 all-gather.3
  178.0 76.9 reduce-scatter.1
where the time goes:
time: 265 us
  waiting for transfers between devices  77.1 us (29%)
  local copies, waits for them, and re-layouts  63.7 us (24%)
  matrix products  62.9 us (24%)
  blocking collectives  24.2 us (9%)
  other arithmetic  22.6 us (9%)
  between operations  14.3 us (5%)
    reduce_scatter x1, waiting for transfers between devices, body(): lax.psum_scatter(partial.astype(jnp.bfloat16), 'tok', scatter_dimension=0...  76.4 us
    unnamed x16, local copies, waits for them, and re-layouts  45.7 us
    dot_general x1, matrix products, body(): jnp.einsum('sbce,sbed->sbcd', all_codes, decoder_weight[0].reshape(layers...  26.1 us
    dot_general x1, matrix products, body(): jnp.einsum('sct,scd->td', scatter.astype(jnp.bfloat16), terms.reshape(lay...  21.6 us
    another operation x3, other arithmetic  19 us
    dot_general x1, matrix products, body(): jnp.einsum('bcd,dbe->bce', rows.reshape(per_owner, capacity, width), enc_...  15.1 us
    all_gather x1, blocking collectives, body(): ids_all = lax.all_gather(block_ids, 'tok', axis=1, tiled=True)  13.8 us
    gather x1, local copies, waits for them, and re-layouts, body(): rows = jnp.take(res_all, jnp.minimum(own_table, tokens - 1), axis=0)  12 us
  transfers between devices with their start and end apart: 2, of which 1 were waited for; matrix products, arithmetic and copies ran while one was open for 27% of the time, Pallas kernels for 0%

commit v1 on v0

--- a/solution.py
+++ b/solution.py
@@ -32,7 +32,27 @@
     capacity = max(2, 2 * tok_rows * topk // blocks) * tok_count
     slot_count = per_owner * capacity
     tokens = tok_rows * tok_count
-    ids_all = lax.all_gather(block_ids, "tok", axis=1, tiled=True)
+    part_now = lax.axis_size("tok")
+    base_arr = lax.axis_index("tok")
+    reached, extra, block_next = (part_now, base_arr, block_ids.shape[1])
+    buffers = [(nth, (nth + 1) % reached) for nth in range(reached)]
+    row_list = [(nth, (nth - 1) % reached) for nth in range(reached)]
+    ids_all = jnp.zeros(
+        (*block_ids.shape[:1], reached * block_next, *block_ids.shape[2:]), block_ids.dtype
+    )
+    ids_all = lax.dynamic_update_slice_in_dim(ids_all, block_ids, extra * block_next, axis=1)
+    local_now = all_rows = block_ids
+    o_now = reached // 2
+    for ix in [*range(1, o_now + 1)]:
+        local_now = lax.ppermute(local_now, "tok", buffers)
+        ids_all = lax.dynamic_update_slice_in_dim(
+            ids_all, local_now, (extra - ix) % reached * block_next, axis=1
+        )
+        if ix < reached - o_now:
+            all_rows = lax.ppermute(all_rows, "tok", perm=row_list)
+            ids_all = lax.dynamic_update_slice_in_dim(
+                ids_all, all_rows, (extra + ix) % reached * block_next, axis=1
+            )
     table = owner_tables(ids_all, tok_index, per_owner, capacity, tokens)
     res_all = lax.all_gather(residual[0], "tok", axis=0, tiled=True)
     own_table = lax.dynamic_index_in_dim(table, layer_index, 0, keepdims=False)

time: 265 us -> 278 us (1.049)
  blocking collectives: 24.2 us -> 10.5 us
  starting transfers between devices: 0.08 us -> 12 us
  local copies, waits for them, and re-layouts: 63.7 us -> 71.1 us
  other arithmetic: 22.6 us -> 26.1 us
  waiting for transfers between devices: 77.1 us -> 80.6 us
    all_gather x1 -> x0, blocking collectives: 13.8 us -> none  [body(): ids_all = lax.all_gather(block_ids, 'tok', axis=1, tiled=True)]
    ppermute x0 -> x7, starting transfers between devices: none -> 11.9 us  [the longest x3 11.3 us: body(): all_rows = lax.ppermute(all_rows, 'tok', perm=row_list)]
    dynamic_update_slice x0 -> x8, local copies, waits for them, and re-layouts: none -> 5.29 us  [the longest x4 2.65 us: body(): lax.dynamic_update_slice_in_dim(ids_all, local_now, (extra - ix) % reache...]
    ppermute x0 -> x7, waiting for transfers between devices: none -> 3.49 us  [the longest x4 3.48 us: body(): local_now = lax.ppermute(local_now, 'tok', buffers)]
    unnamed x16 -> x17, local copies, waits for them, and re-layouts: 45.7 us -> 46.7 us
  transfers between devices with their start and end apart: 2 -> 9, of which waited for: 1 -> 2; matrix products, arithmetic and copies ran while one was open for 27% -> 29% of each run, Pallas kernels for 0% -> 0%
where the time goes in v1:
time: 278 us
  waiting for transfers between devices  80.6 us (29%)
  local copies, waits for them, and re-layouts  71.1 us (26%)
  matrix products  62.9 us (23%)
  other arithmetic  26.1 us (9%)
  between operations  14.4 us (5%)
  starting transfers between devices  12 us (4%)
  blocking collectives  10.5 us (4%)
    reduce_scatter x1, waiting for transfers between devices, body(): lax.psum_scatter(partial.astype(jnp.bfloat16), 'tok', scatter_dimension=0...  76.4 us
    unnamed x17, local copies, waits for them, and re-layouts  46.7 us
    dot_general x1, matrix products, body(): jnp.einsum('sbce,sbed->sbcd', all_codes, decoder_weight[0].reshape(layers...  26.1 us
    dot_general x1, matrix products, body(): jnp.einsum('sct,scd->td', scatter.astype(jnp.bfloat16), terms.reshape(lay...  21.6 us
    another operation x3, other arithmetic  19.8 us
    dot_general x1, matrix products, body(): jnp.einsum('bcd,dbe->bce', rows.reshape(per_owner, capacity, width), enc_...  15.1 us
    gather x1, local copies, waits for them, and re-layouts, body(): rows = jnp.take(res_all, jnp.minimum(own_table, tokens - 1), axis=0)  12.2 us
    ppermute x3, starting transfers between devices, body(): all_rows = lax.ppermute(all_rows, 'tok', perm=row_list)  11.3 us
  transfers between devices with their start and end apart: 9, of which 2 were waited for; matrix products, arithmetic and copies ran while one was open for 29% of the time, Pallas kernels for 0%

profile of v1, /device:TPU:0, one launch (start us, length us, event | category | flops | bytes accessed | tf_op | source)
XLA Modules:
  0.0 277.5 jit_solution(16243504404873140338)
XLA Ops:
  7.2 0.0 all-gather.4.cloned.1.call-start
  7.2 0.7 all-gather.4.cloned.1.call-update
  7.9 0.0 reduce-scatter.2.cloned.1.call-start
  7.9 0.5 collective-permute-start
  8.4 4.1 %collective-permute-start.1 = (s32[4,128,2]{1,2,0:T(2,128)}, s32[4,128,2]{1,2,0:T(2,128)S(1)}, u32[]{:S(2)}, u32[]{:S(2)}) collective-permute-start(s32[4,128,2]{1,2,0:T(2,128)} %param.9), channel_id=1, source_target_pairs={{0,7},{1,0},{2,1},{3,2},{4,3},{5,4},{6,5},{7,6},{8,15},{9,8},{10,9... | collective-permute-start | bytes 12296 | tf_op jit(solution)/shard_map/ppermute | solution.py:52
  12.6 0.9 copy.23
  13.5 1.3 broadcast_in_dim.30
  14.8 0.7 constant_dynamic-update-slice_fusion.7
  15.4 14.7 %copy.39 = bf16[448,8,16,128]{3,2,1,0:T(8,128)(2,1)} copy(bf16[448,8,16,128]{3,1,2,0:T(8,128)(2,1)} %bitcast.55) | data formatting | bytes 29360128
  30.1 0.0 collective-permute-done
  30.1 0.2 copy.24
  30.3 0.1 collective-permute-start.2
  30.3 0.0 collective-permute-done.1
  30.3 0.2 copy.25
  30.5 3.6 %collective-permute-start.3 = (s32[4,128,2]{1,2,0:T(2,128)S(1)}, s32[4,128,2]{1,2,0:T(2,128)S(1)}, u32[]{:S(2)}, u32[]{:S(2)}) collective-permute-start(s32[4,128,2]{1,2,0:T(2,128)S(1)} %collective-permute-done.1), channel_id=1, source_target_pairs={{0,7},{1,0},{2,1},{3,2},{4,3},{5,4},{6,5},{7,6},{8,15},{9,8},{10,9... | collective-permute-start | bytes 12296 | tf_op jit(solution)/shard_map/ppermute | solution.py:52
  34.1 0.7 constant_dynamic-update-slice_fusion.6
  34.7 0.7 constant_dynamic-update-slice_fusion.5
  35.4 0.0 collective-permute-done.2
  35.4 0.2 copy.26
  35.6 0.1 collective-permute-start.4
  35.6 0.0 collective-permute-done.3
  35.6 0.2 copy.27
  35.8 3.6 %collective-permute-start.5 = (s32[4,128,2]{1,2,0:T(2,128)S(1)}, s32[4,128,2]{1,2,0:T(2,128)S(1)}, u32[]{:S(2)}, u32[]{:S(2)}) collective-permute-start(s32[4,128,2]{1,2,0:T(2,128)S(1)} %collective-permute-done.3), channel_id=1, source_target_pairs={{0,7},{1,0},{2,1},{3,2},{4,3},{5,4},{6,5},{7,6},{8,15},{9,8},{10,9... | collective-permute-start | bytes 12296 | tf_op jit(solution)/shard_map/ppermute | solution.py:52
  39.4 0.7 constant_dynamic-update-slice_fusion.4
  40.0 0.7 constant_dynamic-update-slice_fusion.3
  40.7 0.2 copy.28
  40.9 0.1 collective-permute-start.6
  40.9 0.0 collective-permute-done.5
  40.9 0.2 copy.29
  41.1 0.7 constant_dynamic-update-slice_fusion.2
  41.8 0.7 constant_dynamic-update-slice_fusion.1
  42.4 3.5 %collective-permute-done.6 = s32[4,128,2]{1,2,0:T(2,128)S(1)} collective-permute-done((s32[4,128,2]{1,2,0:T(2,128)S(1)}, s32[4,128,2]{1,2,0:T(2,128)S(1)}, u32[]{:S(2)}, u32[]{:S(2)}) %collective-permute-start.6) | collective-permute-done | bytes 4128 | tf_op jit(solution)/shard_map/ppermute | solution.py:47
  45.9 0.2 copy.30
  46.1 0.7 constant_dynamic-update-slice_fusion
  46.7 1.9 broadcast_multiply_fusion
  48.6 0.3 copy.33
  48.9 0.1 fusion.30
  49.0 18.1 %reduce-window.6 = s32[4,16,16,128]{3,2,1,0:T(8,128)S(1)} reduce-window(s32[4,16,16,128]{3,2,1,0:T(8,128)S(1)} %fusion.30, s32[]{:T(128)} %constant.97.clone.1), window={size=1x1x1x128 pad=0_0x0_0x0_0x127_0}, to_apply=%region_0.1 | reduce-window | flops 16646144 | bytes 1048580 | tf_op jit(solution)/shard_map/reduce-window
  67.1 1.3 slice_reduce_fusion
  68.5 0.7 reduce-window.9
  69.1 1.0 broadcast_add_fusion
  70.2 1.2 reduce_window_sum.16
  71.3 0.3 copy.32
  71.6 0.8 compare_and_fusion
  72.5 0.7 reshape.155
  73.1 0.4 copy.36
  73.5 0.3 copy.34
  73.8 0.2 fusion.29
  74.1 0.1 multiply_reduce_fusion
  74.2 0.1 and_reduce_fusion
  74.3 30.4 %scatter_custom_fusion = s32[2048]{0:T(1024)S(1)} fusion(s32[8192]{0:T(1024)S(1)} %bitcast.62, s32[8192]{0:T(1024)S(1)} %bitcast.61, s32[]{:T(128)} %constant.96.clone.1), kind=kCustom, calls=%fused_computation.52 | custom fusion | bytes 8196
  104.8 0.1 min.26
  104.9 0.0 all-gather.4.cloned.1.call-done
  104.9 0.0 copy-start.4
  105.0 12.2 %gather_fusion = bf16[512,3584]{1,0:T(8,128)(2,1)} fusion(bf16[1024,3584]{1,0:T(8,128)(2,1)} %bitcast.50, s32[1024]{0:T(1024)S(1)} %pad_clamp_fusion), kind=kCustom, calls=%fused_computation | custom fusion | bytes 7342080 | tf_op jit(solution)/shard_map/jit(_take)/gather | solution.py:59
  117.1 15.1 %fusion.22 = bf16[16,32,128]{2,1,0:T(8,128)(2,1)S(1)} fusion(bf16[3584,16,128]{2,1,0:T(8,128)(2,1)} %bitcast.56, bf16[16,32,3584]{2,1,0:T(8,128)(2,1)} %bitcast.58, pred[16,32]{1,0:T(8,128)(4,1)S(1)} %compare_and_fusion.1, f32[16,128]{1,0:T(8,128)S(1)} %bitcast.64), kind=kOutput, calls=%fused_computation.21 | convolution fusion | flops 471793664 | bytes 18489856 | tf_op jit(solution)/shard_map/bcd,dbe->bce/dot_general | solution.py:61
  132.3 10.5 %all-gather.1 = bf16[64,32,128]{2,1,0:T(8,128)(2,1)S(1)} all-gather(bf16[16,32,128]{2,1,0:T(8,128)(2,1)S(1)} %fusion.22), channel_id=3, replica_groups=mesh['layer'=4,'tok'=8] {'layer'}, dimensions={0}, use_global_device_ids=true | all-gather | bytes 655360 | tf_op jit(solution)/shard_map/all_gather | solution.py:69
  142.8 26.1 %convolution_convert_fusion = bf16[4,16,32,3584]{3,2,1,0:T(8,128)(2,1)} fusion(bf16[4,16,32,128]{3,2,1,0:T(8,128)(2,1)S(1)} %bitcast.59, bf16[4,16,128,3584]{3,2,1,0:T(8,128)(2,1)} %bitcast.51), kind=kOutput, calls=%fused_computation.5 | convolution fusion | flops 1886388224 | bytes 73924608 | tf_op jit(solution)/shard_map/sbce,sbed->sbcd/dot_general | solution.py:70
  168.9 21.6 %bitcast_convert_fusion = bf16[1024,3584]{1,0:T(8,128)(2,1)} fusion(bf16[4,512,3584]{2,1,0:T(8,128)(2,1)} %bitcast.52, s32[4,512]{1,0:T(4,128)S(1)} %reshape.136, pred[4]{0:T(512)(128)(4,1)S(1)} %iota_compare_fusion.3), kind=kOutput, calls=%fused_computation.2 | convolution fusion | flops 15040249856 | bytes 22028292 | tf_op jit(solution)/shard_map/sct,scd->td/dot_general | solution.py:80
  190.5 0.0 reduce-scatter.2.cloned.1.call-update
  190.5 0.7 copy-done.1
  191.3 76.4 %reduce-scatter.2.cloned.1.call-done = bf16[128,3584]{1,0:T(8,128)(2,1)} async-done(((bf16[1024,3584]{1,0:T(8,128)(2,1)}), bf16[128,3584]{1,0:T(8,128)(2,1)}) %reduce-scatter.2.cloned.1.call-update) | async-done | bytes 917520 | tf_op jit(solution)/shard_map/reduce_scatter | solution.py:86
  267.7 2.5 fusion.9
  270.2 0.5 multiply_bitcast_fusion
  (23 shorter events, 0.2 us)
Async XLA Ops:
  7.2 97.8 %all-gather.4.cloned.1.call-start = ((), (), s32[]{:S(2)}) async-start(), calls=%async_computation.2 | async-start | bytes 8257536 | tf_op jit(solution)/shard_map/all_gather | solution.py:57
  7.9 259.8 %reduce-scatter.2.cloned.1.call-start = ((), (), s32[]{:S(2)}) async-start(), calls=%async_computation.1 | async-start | bytes 8257536 | tf_op jit(solution)/shard_map/reduce_scatter | solution.py:86
  7.9 22.2 %collective-permute-start = (s32[4,128,2]{1,2,0:T(2,128)}, s32[4,128,2]{1,2,0:T(2,128)S(1)}, u32[]{:S(2)}, u32[]{:S(2)}) collective-permute-start(s32[4,128,2]{1,2,0:T(2,128)} %param.9), channel_id=1, source_target_pairs={{0,1},{1,2},{2,3},{3,4},{4,5},{5,6},{6,7},{7,0},{8,9},{9,10},{10,1... | collective-permute-start | bytes 12296 | tf_op jit(solution)/shard_map/ppermute | solution.py:47
  8.4 21.9 %collective-permute-start.1 = (s32[4,128,2]{1,2,0:T(2,128)}, s32[4,128,2]{1,2,0:T(2,128)S(1)}, u32[]{:S(2)}, u32[]{:S(2)}) collective-permute-start(s32[4,128,2]{1,2,0:T(2,128)} %param.9), channel_id=1, source_target_pairs={{0,7},{1,0},{2,1},{3,2},{4,3},{5,4},{6,5},{7,6},{8,15},{9,8},{10,9... | collective-permute-start | bytes 12296 | tf_op jit(solution)/shard_map/ppermute | solution.py:52
  30.3 5.1 %collective-permute-start.2 = (s32[4,128,2]{1,2,0:T(2,128)S(1)}, s32[4,128,2]{1,2,0:T(2,128)S(1)}, u32[]{:S(2)}, u32[]{:S(2)}) collective-permute-start(s32[4,128,2]{1,2,0:T(2,128)S(1)} %collective-permute-done), channel_id=1, source_target_pairs={{0,1},{1,2},{2,3},{3,4},{4,5},{5,6},{6,7},{7,0},{8,9},{9,10},{10,1... | collective-permute-start | bytes 12296 | tf_op jit(solution)/shard_map/ppermute | solution.py:47
  30.5 5.1 %collective-permute-start.3 = (s32[4,128,2]{1,2,0:T(2,128)S(1)}, s32[4,128,2]{1,2,0:T(2,128)S(1)}, u32[]{:S(2)}, u32[]{:S(2)}) collective-permute-start(s32[4,128,2]{1,2,0:T(2,128)S(1)} %collective-permute-done.1), channel_id=1, source_target_pairs={{0,7},{1,0},{2,1},{3,2},{4,3},{5,4},{6,5},{7,6},{8,15},{9,8},{10,9... | collective-permute-start | bytes 12296 | tf_op jit(solution)/shard_map/ppermute | solution.py:52
  35.6 5.1 %collective-permute-start.4 = (s32[4,128,2]{1,2,0:T(2,128)S(1)}, s32[4,128,2]{1,2,0:T(2,128)S(1)}, u32[]{:S(2)}, u32[]{:S(2)}) collective-permute-start(s32[4,128,2]{1,2,0:T(2,128)S(1)} %collective-permute-done.2), channel_id=1, source_target_pairs={{0,1},{1,2},{2,3},{3,4},{4,5},{5,6},{6,7},{7,0},{8,9},{9,10},{10,1... | collective-permute-start | bytes 12296 | tf_op jit(solution)/shard_map/ppermute | solution.py:47
  35.8 5.1 %collective-permute-start.5 = (s32[4,128,2]{1,2,0:T(2,128)S(1)}, s32[4,128,2]{1,2,0:T(2,128)S(1)}, u32[]{:S(2)}, u32[]{:S(2)}) collective-permute-start(s32[4,128,2]{1,2,0:T(2,128)S(1)} %collective-permute-done.3), channel_id=1, source_target_pairs={{0,7},{1,0},{2,1},{3,2},{4,3},{5,4},{6,5},{7,6},{8,15},{9,8},{10,9... | collective-permute-start | bytes 12296 | tf_op jit(solution)/shard_map/ppermute | solution.py:52
  40.9 5.0 %collective-permute-start.6 = (s32[4,128,2]{1,2,0:T(2,128)S(1)}, s32[4,128,2]{1,2,0:T(2,128)S(1)}, u32[]{:S(2)}, u32[]{:S(2)}) collective-permute-start(s32[4,128,2]{1,2,0:T(2,128)S(1)} %collective-permute-done.4), channel_id=1, source_target_pairs={{0,1},{1,2},{2,3},{3,4},{4,5},{5,6},{6,7},{7,0},{8,9},{9,10},{10,1... | collective-permute-start | bytes 12296 | tf_op jit(solution)/shard_map/ppermute | solution.py:47
  41.8 32.3 %copy-start.3 = (s32[2]{0:T(128)S(1)}, s32[2]{0:T(128)}, u32[]{:S(2)}) copy-start(s32[2]{0:T(128)} %constant.124) | copy-start | bytes 28
  42.4 31.7 %copy-start.2 = (s32[2]{0:T(128)S(1)}, s32[2]{0:T(128)}, u32[]{:S(2)}) copy-start(s32[2]{0:T(128)} %constant.127) | copy-start | bytes 28
  104.9 12.2 %copy-start.4 = (f32[1,2048]{1,0:T(1,128)S(1)}, f32[1,2048]{1,0:T(1,128)}, u32[]{:S(2)}) copy-start(f32[1,2048]{1,0:T(1,128)} %param.11) | copy-start | bytes 24580
  190.5 0.7 copy-start.1
  190.5 77.2 %copy-start = (bf16[1,128,3584]{2,1,0:T(8,128)(2,1)S(1)}, bf16[1,128,3584]{2,1,0:T(8,128)(2,1)}, u32[]{:S(2)}) copy-start(bf16[1,128,3584]{2,1,0:T(8,128)(2,1)} %param.8) | copy-start | bytes 2752516
Sparse Core Ops, SparseCore 0:
  9.6 76.3 all-gather.3
  190.7 76.9 reduce-scatter.1
